TPU v7x, 512 devices: a whole 4x8x8 slice. The times are simulated.
512 devices in a mesh: context: 32 (over x_hi, y, core), tensor: 16 (over z, x_lo).
Axes of the slice: x: 4 (x_hi: 2, x_lo: 2; x = x_hi * 2 + x_lo), y: 8, z: 8, core: 2. Of those that a mesh axis runs over, the one named last changes fastest.
Arguments:
- projected: bfloat16 [3, 12288, 8192], P(None, 'context', 'tensor'), may hold values from -6 to 6
- taps: float32 [3, 3, 8192], P(None, None, 'tensor'), may hold values from -4 to 4
- filters: bfloat16 [512, 128], P('tensor'), may hold values from -0.5 to 0.5
- skip: float32 [8192], P('tensor'), may hold values from -4 to 4
- out_weight: bfloat16 [8192, 8192], P('tensor', 'context'), may hold values from -0.125 to 0.125
- positions: int32 [128], replicated, may hold values from 0 to 12287
Outputs:
- mixed: bfloat16 [12288, 8192], P('context', 'tensor')
- variant_states: bfloat16 [128, 8192], P('context', 'tensor')
All inputs are finite; a program needn't handle non-finite values.
Results may differ from a plain program's by a relative error of at most 0.018.
Values may be sent and summed in bfloat16 or wider, within the bound.
No kernel may reach another device: no remote copies, remote signals or barrier semaphores. Data moves between devices by JAX's collectives and lax.ppermute only.
A program may use at most 128 MiB of HBM per device.

v0:
```python
import jax
import jax.numpy as jnp
from jax import lax
import numpy as np
from jax.sharding import Mesh, PartitionSpec as P

FLT = 128
GROUP = 16
SHORT = 3


def shifted(array, axis, by):
    size = lax.axis_size(axis)
    pairs = [(i, i + by) for i in range(size) if 0 <= i + by < size]
    return lax.ppermute(array, axis, pairs)


def pair_scatter(block, axis):
    me = lax.axis_index(axis)
    half = block.shape[1] // 2
    keep = lax.dynamic_slice_in_dim(block, me * half, half, 1)
    send = lax.dynamic_slice_in_dim(block, (1 - me) * half, half, 1)
    got = lax.ppermute(send, axis, [(0, 1), (1, 0)])
    return (keep.astype(jnp.float32) + got.astype(jnp.float32)).astype(block.dtype)


def exchange_scatter(rows, axis):
    size = lax.axis_size(axis)
    pieces = rows.reshape(size, rows.shape[0] // size, rows.shape[1])
    pieces = lax.all_to_all(pieces, axis, 0, 0, tiled=True)
    return pieces.astype(jnp.float32).sum(0).astype(rows.dtype)


def short_filter(extended, weights, count):
    lags = SHORT - 1
    total = jnp.zeros((extended.shape[0], count, extended.shape[2]), jnp.float32)
    for lag in range(SHORT):
        total = total + weights[:, lag, None, :] * extended[
            :, lags - lag : lags - lag + count, :
        ].astype(jnp.float32)
    return total


def banded_filters(filters, rows):
    local_groups = filters.shape[0]
    span = FLT - 1 + rows
    reversed_taps = jnp.flip(filters, axis=1)
    padded_taps = jnp.concatenate(
        [reversed_taps, jnp.zeros((local_groups, rows), filters.dtype)], axis=1
    )
    tiled = jnp.tile(padded_taps, (1, rows))
    return tiled[:, : rows * span].reshape(local_groups, rows, span)


def on_device(projected, taps, filters, skip, out_weight, positions):
    rows = projected.shape[1]
    width = projected.shape[2]
    lags = SHORT - 1
    reach = FLT - 1
    rim = shifted(projected[:, rows - lags :, :], "context", 1)
    feat = short_filter(jnp.concatenate([rim, projected], axis=1), taps, rows)
    query = feat[0]
    product = (feat[1] * feat[2]).astype(jnp.bfloat16)
    prior = shifted(product[rows - reach :], "context", 1)
    extended = jnp.concatenate([prior, product], axis=0)
    span = reach + rows
    toeplitz = banded_filters(filters, rows)
    local_groups = filters.shape[0]
    conv = jnp.einsum(
        "gim,mgc->igc",
        toeplitz,
        extended.reshape(span, local_groups, GROUP),
        preferred_element_type=jnp.float32,
    ).reshape(rows, width)
    conv = conv + skip[None, :] * product.astype(jnp.float32)
    gated = lax.optimization_barrier((query * conv).astype(jnp.bfloat16))
    offset = lax.axis_index("context") * rows
    local_sites = positions - offset
    one_hot = (local_sites[:, None] == jnp.arange(rows, dtype=jnp.int32)[None, :]).astype(
        jnp.bfloat16
    )
    picked_gated = jnp.dot(one_hot, gated, preferred_element_type=jnp.float32)
    site_gated = exchange_scatter(picked_gated.astype(jnp.bfloat16), "context")
    gated, site_gated = lax.optimization_barrier((gated, site_gated))
    full_weight = lax.all_gather(out_weight, "context", axis=1, tiled=True)
    sites = site_gated.shape[0]
    padding = jnp.zeros((-(rows + sites) % 8, width), gated.dtype)
    both = lax.optimization_barrier(jnp.concatenate([gated, site_gated, padding], axis=0))
    both = jnp.dot(both, full_weight, preferred_element_type=jnp.float32).astype(jnp.bfloat16)
    partial = lax.psum_scatter(both, "z", scatter_dimension=1, tiled=True)
    reduced = pair_scatter(partial, "x_lo")
    mixed = reduced[:rows]
    variant_states = reduced[rows : rows + sites]
    return (mixed, variant_states)


def split_mesh(mesh):
    devices = np.asarray(mesh.devices)
    context, tensor = devices.shape
    return Mesh(devices.reshape(context, tensor // 2, 2), ("context", "z", "x_lo"))


def solution(mesh):
    tensor = ("z", "x_lo")
    return jax.shard_map(
        on_device,
        mesh=split_mesh(mesh),
        in_specs=(
            P(None, "context", tensor),
            P(None, None, tensor),
            P(tensor, None),
            P(tensor),
            P(tensor, "context"),
            P(),
        ),
        out_specs=(P("context", tensor), P("context", tensor)),
        check_vma=False,
    )
```

profile of v0, /device:TPU:1, one launch (start us, length us, event | category | flops | bytes accessed | tf_op | source)
XLA Modules:
  0.0 241.7 jit_solution(7688944672993362209)
XLA Ops:
  7.2 0.0 all-gather.2.cloned.1.call-start
  7.2 0.7 all-gather.2.cloned.1.call-update
  7.9 0.8 slice.44
  8.7 4.6 %collective-permute-start = (bf16[3,2,512]{2,1,0:T(2,128)(2,1)S(1)}, bf16[3,2,512]{2,1,0:T(2,128)(2,1)S(1)}, u32[]{:S(2)}, u32[]{:S(2)}) collective-permute-start(bf16[3,2,512]{2,1,0:T(2,128)(2,1)S(1)} %slice.44), channel_id=1, source_target_pairs={{0,16},{16,32},{32,48},{48,64},{64,80},{80,96},{96,112},{112,128},... | collective-permute-start | bytes 18440 | tf_op jit(solution)/shard_map/ppermute | solution.py:15
  13.3 0.9 fusion.5
  14.1 1.2 broadcast_subtract_fusion
  15.3 0.6 copy.19
  15.9 0.8 rev.4
  16.7 5.4 %tile.4 = bf16[32,384,512]{2,1,0:T(8,128)(2,1)} broadcast(bf16[32,512]{1,0:T(8,128)(2,1)S(1)} %concatenate.14), dimensions={0,2} | broadcast | bytes 12615680 | tf_op jit(solution)/shard_map/tile | solution.py:51
  22.1 12.0 %copy.15 = bf16[4,8,384,512]{3,1,2,0:T(8,128)(2,1)S(1)} copy(bf16[4,8,384,512]{3,2,1,0:T(8,128)(2,1)} %bitcast.29) | data formatting | bytes 25165824
  34.2 5.2 %slice.62 = bf16[32,196224]{1,0:T(8,128)(2,1)} slice(bf16[32,196608]{1,0:T(8,128)(2,1)S(1)} %bitcast.30), slice={[0:32], [0:196224]} | slice | bytes 25116672 | tf_op jit(solution)/shard_map/slice | solution.py:52
  39.3 0.0 copy-start
  39.3 29.3 %reshape.26 = bf16[32,384,511]{2,1,0:T(8,128)(2,1)} reshape(bf16[32,196224]{1,0:T(8,128)(2,1)} %slice.62) | data formatting | bytes 25116672 | tf_op jit(solution)/shard_map/reshape | solution.py:52
  68.7 0.0 collective-permute-done
  68.7 0.0 copy-start.1
  68.7 0.6 copy-done.1
  69.3 0.0 copy-done
  69.3 1.5 multiply_add_fusion
  70.8 0.1 fusion.1
  71.0 2.1 collective-permute-start.1
  73.1 0.1 fusion.12
  73.2 3.4 %collective-permute-done.1 = bf16[127,512]{1,0:T(8,128)(2,1)S(1)} collective-permute-done((bf16[127,512]{1,0:T(8,128)(2,1)S(1)}, bf16[127,512]{1,0:T(8,128)(2,1)S(1)}, u32[]{:S(2)}, u32[]{:S(2)}) %collective-permute-start.1) | collective-permute-done | bytes 130080 | tf_op jit(solution)/shard_map/ppermute | solution.py:15
  76.6 0.1 pad_maximum_fusion.1
  76.7 0.2 copy.10
  76.9 0.0 copy-start.2
  76.9 9.0 %fusion.6 = f32[32,16,384]{2,1,0:T(8,128)} fusion(bf16[511,32,16]{0,2,1:T(8,128)(2,1)S(1)} %bitcast.32, bf16[32,384,511]{2,1,0:T(8,128)(2,1)} %reshape.26), kind=kOutput, calls=%fused_computation.24 | convolution fusion | flops 200933376 | bytes 13868032 | tf_op jit(solution)/shard_map/gim,mgc->igc/dot_general | solution.py:69
  86.0 1.4 copy.11
  87.4 0.0 copy-done.2
  87.4 0.4 fusion.3
  87.8 0.0 copy-done.3
  87.8 0.3 convolution_convert_fusion.1
  88.1 0.7 reshape.28
  88.8 12.8 %all-to-all-start = ((bf16[32,4,512]{2,1,0:T(4,128)(2,1)}), bf16[32,4,512]{2,1,0:T(4,128)(2,1)S(1)}, u32[]{:S(2)}, u32[]{:S(2)}) async-start(bf16[32,4,512]{2,1,0:T(4,128)(2,1)} %reshape.28), calls=%async_computation | async-start | bytes 262144 | tf_op jit(solution)/shard_map/all_to_all | solution.py:30
  101.5 0.0 reduce-scatter.2.cloned.1.call-start
  101.6 0.1 pad.3.clone
  101.7 10.8 %all-to-all-done = bf16[32,4,512]{2,1,0:T(4,128)(2,1)S(1)} async-done(((bf16[32,4,512]{2,1,0:T(4,128)(2,1)}), bf16[32,4,512]{2,1,0:T(4,128)(2,1)S(1)}, u32[]{:S(2)}, u32[]{:S(2)}) %all-to-all-start) | async-done | bytes 131104 | tf_op jit(solution)/shard_map/all_to_all | solution.py:30
  112.4 0.1 reduce_sum.12
  112.5 0.1 maximum_maximum_fusion
  112.6 20.2 %all-gather.2.cloned.1.call-done = bf16[512,8192]{1,0:T(8,128)(2,1)} async-done(((bf16[512,256]{1,0:T(8,128)(2,1)}), bf16[512,8192]{1,0:T(8,128)(2,1)}) %all-gather.2.cloned.1.call-update) | async-done | bytes 8388624 | tf_op jit(solution)/shard_map/all_gather | solution.py:85
  132.8 8.9 %convolution_convert_fusion = bf16[392,8192]{1,0:T(8,128)(2,1)} fusion(bf16[392,512]{1,0:T(8,128)(2,1)S(1)} %maximum_maximum_fusion, bf16[512,8192]{1,0:T(8,128)(2,1)} %all-gather.2.cloned.1.call-done), kind=kOutput, calls=%fused_computation | convolution fusion | flops 3291545600 | bytes 15212544 | tf_op jit(solution)/shard_map/dot_general | solution.py:89
  141.7 0.0 reduce-scatter.2.cloned.1.call-update
  141.7 77.5 %reduce-scatter.2.cloned.1.call-done = bf16[392,1024]{1,0:T(8,128)(2,1)} async-done(((bf16[392,8192]{1,0:T(8,128)(2,1)}), bf16[392,1024]{1,0:T(8,128)(2,1)}) %reduce-scatter.2.cloned.1.call-update) | async-done | bytes 802832 | tf_op jit(solution)/shard_map/reduce_scatter | solution.py:90
  219.2 1.0 constant_dynamic-slice_fusion
  220.3 3.1 %collective-permute-start.2 = (bf16[392,512]{1,0:T(8,128)(2,1)S(1)}, bf16[392,512]{1,0:T(8,128)(2,1)S(1)}, u32[]{:S(2)}, u32[]{:S(2)}) collective-permute-start(bf16[392,512]{1,0:T(8,128)(2,1)S(1)} %constant_dynamic-slice_fusion), channel_id=1, source_target_pairs={{0,1},{1,0},{2,3},{3,2},{4,5},{5,4},{6,7},{7,6},{8,9},{9,8},{10,11... | collective-permute-start | bytes 1204232 | tf_op jit(solution)/shard_map/ppermute | solution.py:23
  223.4 9.0 %collective-permute-done.2 = bf16[392,512]{1,0:T(8,128)(2,1)S(1)} collective-permute-done((bf16[392,512]{1,0:T(8,128)(2,1)S(1)}, bf16[392,512]{1,0:T(8,128)(2,1)S(1)}, u32[]{:S(2)}, u32[]{:S(2)}) %collective-permute-start.2) | collective-permute-done | bytes 401440 | tf_op jit(solution)/shard_map/ppermute | solution.py:23
  232.4 1.1 add_convert_fusion
  233.5 0.8 slice.63
  234.2 0.6 slice.64
  (5 shorter events, 0.1 us)
Async XLA Ops:
  7.2 125.6 %all-gather.2.cloned.1.call-start = ((), (), s32[]{:S(2)}) async-start(), calls=%async_computation.2 | async-start | bytes 8650752 | tf_op jit(solution)/shard_map/all_gather | solution.py:85
  8.7 60.0 %collective-permute-start = (bf16[3,2,512]{2,1,0:T(2,128)(2,1)S(1)}, bf16[3,2,512]{2,1,0:T(2,128)(2,1)S(1)}, u32[]{:S(2)}, u32[]{:S(2)}) collective-permute-start(bf16[3,2,512]{2,1,0:T(2,128)(2,1)S(1)} %slice.44), channel_id=1, source_target_pairs={{0,16},{16,32},{32,48},{48,64},{64,80},{80,96},{96,112},{112,128},... | collective-permute-start | bytes 18440 | tf_op jit(solution)/shard_map/ppermute | solution.py:15
  39.3 29.9 %copy-start = (bf16[3,384,512]{2,1,0:T(8,128)(2,1)S(1)}, bf16[3,384,512]{2,1,0:T(8,128)(2,1)}, u32[]{:S(2)}) copy-start(bf16[3,384,512]{2,1,0:T(8,128)(2,1)} %param.6) | copy-start | bytes 3538948
  68.7 0.6 copy-start.1
  71.0 5.7 %collective-permute-start.1 = (bf16[127,512]{1,0:T(8,128)(2,1)S(1)}, bf16[127,512]{1,0:T(8,128)(2,1)S(1)}, u32[]{:S(2)}, u32[]{:S(2)}) collective-permute-start(bf16[127,512]{1,0:T(8,128)(2,1)S(1)} %slice_bitcast_fusion.1), channel_id=1, source_target_pairs={{0,16},{16,32},{32,48},{48,64},{64,80},{80,96},{96,112},{112,128},... | collective-permute-start | bytes 390152 | tf_op jit(solution)/shard_map/ppermute | solution.py:15
  76.9 10.4 %copy-start.2 = (f32[512]{0:T(512)S(1)}, f32[512]{0:T(512)}, u32[]{:S(2)}) copy-start(f32[512]{0:T(512)} %param.9) | copy-start | bytes 6148
  86.0 1.8 copy-start.3
  88.8 23.7 %all-to-all-start = ((bf16[32,4,512]{2,1,0:T(4,128)(2,1)}), bf16[32,4,512]{2,1,0:T(4,128)(2,1)S(1)}, u32[]{:S(2)}, u32[]{:S(2)}) async-start(bf16[32,4,512]{2,1,0:T(4,128)(2,1)} %reshape.28), calls=%async_computation | async-start | bytes 262144 | tf_op jit(solution)/shard_map/all_to_all | solution.py:30
  101.5 117.7 %reduce-scatter.2.cloned.1.call-start = ((), (), s32[]{:S(2)}) async-start(), calls=%async_computation.3 | async-start | bytes 7225344 | tf_op jit(solution)/shard_map/reduce_scatter | solution.py:90
  220.3 12.1 %collective-permute-start.2 = (bf16[392,512]{1,0:T(8,128)(2,1)S(1)}, bf16[392,512]{1,0:T(8,128)(2,1)S(1)}, u32[]{:S(2)}, u32[]{:S(2)}) collective-permute-start(bf16[392,512]{1,0:T(8,128)(2,1)S(1)} %constant_dynamic-slice_fusion), channel_id=1, source_target_pairs={{0,1},{1,0},{2,3},{3,2},{4,5},{5,4},{6,7},{7,6},{8,9},{9,8},{10,11... | collective-permute-start | bytes 1204232 | tf_op jit(solution)/shard_map/ppermute | solution.py:23
Sparse Core Ops, SparseCore 0:
  11.1 121.6 all-gather.1
  141.8 77.3 reduce-scatter.1
where the time goes:
time: 242 us
  waiting for transfers between devices  122 us (50%)
  local copies, waits for them, and re-layouts  60.4 us (25%)
  starting transfers between devices  22.6 us (9%)
  matrix products  18.2 us (8%)
  between operations  14.2 us (6%)
  other arithmetic  4.73 us (2%)
    reduce_scatter x1, waiting for transfers between devices, on_device(): partial = lax.psum_scatter(both, 'z', scatter_dimension=1, tiled=True)  77.5 us
    reshape x1, local copies, waits for them, and re-layouts, banded_filters(): return tiled[:, :rows * span].reshape(local_groups, rows, span)  29.3 us
    all_gather x1, waiting for transfers between devices, on_device(): full_weight = lax.all_gather(out_weight, 'context', axis=1, tiled=True)  20.2 us
    unnamed x11, local copies, waits for them, and re-layouts  13.2 us
    all_to_all x1, starting transfers between devices, exchange_scatter(): pieces = lax.all_to_all(pieces, axis, 0, 0, tiled=True)  12.8 us
    all_to_all x1, waiting for transfers between devices, exchange_scatter(): pieces = lax.all_to_all(pieces, axis, 0, 0, tiled=True)  10.8 us
    dot_general x1, matrix products, on_device(): jnp.einsum('gim,mgc->igc', toeplitz, extended.reshape(span, local_groups,...  9.02 us
    ppermute x1, waiting for transfers between devices, pair_scatter(): got = lax.ppermute(send, axis, [(0, 1), (1, 0)])  9 us
  transfers between devices with their start and end apart: 6, of which 5 were waited for; matrix products, arithmetic and copies ran while one was open for 29% of the time, Pallas kernels for 0%

commit v1 on v0

--- a/solution.py
+++ b/solution.py
@@ -82,7 +82,8 @@
     picked_gated = jnp.dot(one_hot, gated, preferred_element_type=jnp.float32)
     site_gated = exchange_scatter(picked_gated.astype(jnp.bfloat16), "context")
     gated, site_gated = lax.optimization_barrier((gated, site_gated))
-    full_weight = lax.all_gather(out_weight, "context", axis=1, tiled=True)
+    sent = jnp.stack([out_weight] * lax.axis_size("context"))
+    full_weight = jnp.concatenate(lax.all_to_all(sent, "context", 0, 0), axis=1)
     sites = site_gated.shape[0]
     padding = jnp.zeros((-(rows + sites) % 8, width), gated.dtype)
     both = lax.optimization_barrier(jnp.concatenate([gated, site_gated, padding], axis=0))

time: 242 us -> 423 us (1.75)
  waiting for transfers between devices: 122 us -> 292 us
  local copies, waits for them, and re-layouts: 60.4 us -> 65.6 us
    all_to_all x0 -> x1, waiting for transfers between devices: none -> 185 us  [on_device(): full_weight = jnp.concatenate(lax.all_to_all(sent, 'context', 0, 0), axis=1)]
    all_gather x1 -> x0, waiting for transfers between devices: 20.2 us -> none  [on_device(): full_weight = lax.all_gather(out_weight, 'context', axis=1, tiled=True)]
    reduce_scatter x1, waiting for transfers between devices: 77.5 us -> 84.5 us  [on_device(): partial = lax.psum_scatter(both, 'z', scatter_dimension=1, tiled=True)]
    all_to_all x0 -> x1, starting transfers between devices: none -> 6.18 us  [on_device(): full_weight = jnp.concatenate(lax.all_to_all(sent, 'context', 0, 0), axis=1)]
    unnamed x11 -> x12, local copies, waits for them, and re-layouts: 13.2 us -> 14.3 us
  transfers between devices with their start and end apart: 6 -> 6, of which waited for: 5 -> 5; matrix products, arithmetic and copies ran while one was open for 29% -> 13% of each run, Pallas kernels for 0% -> 0%
where the time goes in v1:
time: 423 us
  waiting for transfers between devices  292 us (69%)
  local copies, waits for them, and re-layouts  65.6 us (16%)
  starting transfers between devices  26.4 us (6%)
  matrix products  19.8 us (5%)
  between operations  14.2 us (3%)
  other arithmetic  4.73 us (1%)
    all_to_all x1, waiting for transfers between devices, on_device(): full_weight = jnp.concatenate(lax.all_to_all(sent, 'context', 0, 0), axis=1)  185 us
    reduce_scatter x1, waiting for transfers between devices, on_device(): partial = lax.psum_scatter(both, 'z', scatter_dimension=1, tiled=True)  84.5 us
    reshape x1, local copies, waits for them, and re-layouts, banded_filters(): return tiled[:, :rows * span].reshape(local_groups, rows, span)  29.3 us
    unnamed x12, local copies, waits for them, and re-layouts  14.3 us
    dot_general x1, matrix products, on_device(): jnp.dot(both, full_weight, preferred_element_type=jnp.float32)  10.7 us
    all_to_all x1, starting transfers between devices, exchange_scatter(): pieces = lax.all_to_all(pieces, axis, 0, 0, tiled=True)  10.4 us
    all_to_all x1, waiting for transfers between devices, exchange_scatter(): pieces = lax.all_to_all(pieces, axis, 0, 0, tiled=True)  9.47 us
    ppermute x1, waiting for transfers between devices, pair_scatter(): got = lax.ppermute(send, axis, [(0, 1), (1, 0)])  8.99 us
  transfers between devices with their start and end apart: 6, of which 5 were waited for; matrix products, arithmetic and copies ran while one was open for 13% of the time, Pallas kernels for 0%

profile of v1, /device:TPU:1, one launch (start us, length us, event | category | flops | bytes accessed | tf_op | source)
XLA Modules:
  0.0 422.6 jit_solution(14449504668288775206)
XLA Ops:
  7.2 0.8 slice.44
  7.9 4.6 %collective-permute-start = (bf16[3,2,512]{2,1,0:T(2,128)(2,1)S(1)}, bf16[3,2,512]{2,1,0:T(2,128)(2,1)S(1)}, u32[]{:S(2)}, u32[]{:S(2)}) collective-permute-start(bf16[3,2,512]{2,1,0:T(2,128)(2,1)S(1)} %slice.44), channel_id=1, source_target_pairs={{0,16},{16,32},{32,48},{48,64},{64,80},{80,96},{96,112},{112,128},... | collective-permute-start | bytes 18440 | tf_op jit(solution)/shard_map/ppermute | solution.py:15
  12.5 0.9 fusion.5
  13.4 1.2 broadcast_subtract_fusion
  14.6 0.6 copy.20
  15.2 0.8 rev.4
  16.0 5.5 %tile.4 = bf16[32,384,512]{2,1,0:T(8,128)(2,1)} broadcast(bf16[32,512]{1,0:T(8,128)(2,1)S(1)} %concatenate.14), dimensions={0,2} | broadcast | bytes 12615680 | tf_op jit(solution)/shard_map/tile | solution.py:51
  21.5 12.0 %copy.16 = bf16[4,8,384,512]{3,1,2,0:T(8,128)(2,1)S(1)} copy(bf16[4,8,384,512]{3,2,1,0:T(8,128)(2,1)} %bitcast.32) | data formatting | bytes 25165824
  33.5 5.1 %slice.62 = bf16[32,196224]{1,0:T(8,128)(2,1)} slice(bf16[32,196608]{1,0:T(8,128)(2,1)S(1)} %bitcast.33), slice={[0:32], [0:196224]} | slice | bytes 25116672 | tf_op jit(solution)/shard_map/slice | solution.py:52
  38.6 29.3 %reshape.34 = bf16[32,384,511]{2,1,0:T(8,128)(2,1)} reshape(bf16[32,196224]{1,0:T(8,128)(2,1)} %slice.62) | data formatting | bytes 25116672 | tf_op jit(solution)/shard_map/reshape | solution.py:52
  67.9 0.0 collective-permute-done
  67.9 0.0 copy-start.1
  67.9 0.6 copy-done.1
  68.5 0.0 copy-done
  68.5 1.5 multiply_add_fusion
  70.1 0.1 fusion.1
  70.2 2.1 collective-permute-start.1
  72.3 0.1 fusion.12
  72.4 3.5 collective-permute-done.1
  75.9 0.1 pad_maximum_fusion.1
  76.0 0.2 copy.10
  76.2 0.0 copy-start.2
  76.2 8.9 %fusion.6 = f32[32,16,384]{2,1,0:T(8,128)} fusion(bf16[511,32,16]{0,2,1:T(8,128)(2,1)S(1)} %bitcast.35, bf16[32,384,511]{2,1,0:T(8,128)(2,1)} %reshape.34), kind=kOutput, calls=%fused_computation.24 | convolution fusion | flops 200933376 | bytes 13868032 | tf_op jit(solution)/shard_map/gim,mgc->igc/dot_general | solution.py:69
  85.1 1.4 copy.11
  86.5 0.0 copy-done.2
  86.5 0.4 fusion.3
  86.9 0.0 copy-done.3
  86.9 0.3 convolution_convert_fusion.1
  87.2 0.7 reshape.36
  87.9 10.4 %all-to-all-start = ((bf16[32,4,512]{2,1,0:T(4,128)(2,1)}), bf16[32,4,512]{2,1,0:T(4,128)(2,1)S(1)}, u32[]{:S(2)}, u32[]{:S(2)}) async-start(bf16[32,4,512]{2,1,0:T(4,128)(2,1)} %reshape.36), calls=%async_computation | async-start | bytes 262144 | tf_op jit(solution)/shard_map/all_to_all | solution.py:30
  98.3 1.1 copy.12
  99.4 9.5 %all-to-all-done = bf16[32,4,512]{2,1,0:T(4,128)(2,1)S(1)} async-done(((bf16[32,4,512]{2,1,0:T(4,128)(2,1)}), bf16[32,4,512]{2,1,0:T(4,128)(2,1)S(1)}, u32[]{:S(2)}, u32[]{:S(2)}) %all-to-all-start) | async-done | bytes 131104 | tf_op jit(solution)/shard_map/all_to_all | solution.py:30
  108.8 4.2 stack.2
  113.0 6.2 %all-to-all-start.1 = ((bf16[32,512,256]{1,2,0:T(8,128)(2,1)}), bf16[32,512,256]{1,2,0:T(8,128)(2,1)}, u32[]{:S(2)}, u32[]{:S(2)}) async-start(bf16[32,512,256]{1,2,0:T(8,128)(2,1)} %stack.2), calls=%async_computation.1 | async-start | bytes 16777216 | tf_op jit(solution)/shard_map/all_to_all | solution.py:86
  119.2 0.0 reduce-scatter.2.cloned.1.call-start
  119.3 0.1 pad.3.clone
  119.4 0.1 reduce_sum.12
  119.4 0.1 maximum_maximum_fusion
  119.6 185.3 %all-to-all-done.1 = bf16[32,512,256]{1,2,0:T(8,128)(2,1)} async-done(((bf16[32,512,256]{1,2,0:T(8,128)(2,1)}), bf16[32,512,256]{1,2,0:T(8,128)(2,1)}, u32[]{:S(2)}, u32[]{:S(2)}) %all-to-all-start.1) | async-done | bytes 8388640 | tf_op jit(solution)/shard_map/all_to_all | solution.py:86
  304.9 10.7 %convolution_convert_fusion = bf16[392,8192]{1,0:T(8,128)(2,1)} fusion(bf16[392,512]{1,0:T(8,128)(2,1)S(1)} %maximum_maximum_fusion, bf16[512,8192]{0,1:T(8,128)(2,1)} %bitcast.7), kind=kOutput, calls=%fused_computation | convolution fusion | flops 3291545600 | bytes 15212544 | tf_op jit(solution)/shard_map/dot_general | solution.py:90
  315.6 0.0 reduce-scatter.2.cloned.1.call-update
  315.6 84.5 %reduce-scatter.2.cloned.1.call-done = bf16[392,1024]{1,0:T(8,128)(2,1)} async-done(((bf16[392,8192]{1,0:T(8,128)(2,1)}), bf16[392,1024]{1,0:T(8,128)(2,1)}) %reduce-scatter.2.cloned.1.call-update) | async-done | bytes 802832 | tf_op jit(solution)/shard_map/reduce_scatter | solution.py:91
  400.1 1.0 constant_dynamic-slice_fusion
  401.1 3.1 collective-permute-start.2
  404.2 9.0 %collective-permute-done.2 = bf16[392,512]{1,0:T(8,128)(2,1)S(1)} collective-permute-done((bf16[392,512]{1,0:T(8,128)(2,1)S(1)}, bf16[392,512]{1,0:T(8,128)(2,1)S(1)}, u32[]{:S(2)}, u32[]{:S(2)}) %collective-permute-start.2) | collective-permute-done | bytes 401440 | tf_op jit(solution)/shard_map/ppermute | solution.py:23
  413.2 1.1 add_convert_fusion
  414.3 0.8 slice.63
  415.1 0.6 slice.64
  (6 shorter events, 0.1 us)
Async XLA Ops:
  7.9 60.0 %collective-permute-start = (bf16[3,2,512]{2,1,0:T(2,128)(2,1)S(1)}, bf16[3,2,512]{2,1,0:T(2,128)(2,1)S(1)}, u32[]{:S(2)}, u32[]{:S(2)}) collective-permute-start(bf16[3,2,512]{2,1,0:T(2,128)(2,1)S(1)} %slice.44), channel_id=1, source_target_pairs={{0,16},{16,32},{32,48},{48,64},{64,80},{80,96},{96,112},{112,128},... | collective-permute-start | bytes 18440 | tf_op jit(solution)/shard_map/ppermute | solution.py:15
  38.6 29.9 %copy-start = (bf16[3,384,512]{2,1,0:T(8,128)(2,1)S(1)}, bf16[3,384,512]{2,1,0:T(8,128)(2,1)}, u32[]{:S(2)}) copy-start(bf16[3,384,512]{2,1,0:T(8,128)(2,1)} %param.6) | copy-start | bytes 3538948
  67.9 0.6 copy-start.1
  70.2 5.7 %collective-permute-start.1 = (bf16[127,512]{1,0:T(8,128)(2,1)S(1)}, bf16[127,512]{1,0:T(8,128)(2,1)S(1)}, u32[]{:S(2)}, u32[]{:S(2)}) collective-permute-start(bf16[127,512]{1,0:T(8,128)(2,1)S(1)} %slice_bitcast_fusion.1), channel_id=1, source_target_pairs={{0,16},{16,32},{32,48},{48,64},{64,80},{80,96},{96,112},{112,128},... | collective-permute-start | bytes 390152 | tf_op jit(solution)/shard_map/ppermute | solution.py:15
  76.2 10.3 %copy-start.2 = (f32[512]{0:T(512)S(1)}, f32[512]{0:T(512)}, u32[]{:S(2)}) copy-start(f32[512]{0:T(512)} %param.9) | copy-start | bytes 6148
  85.1 1.8 copy-start.3
  87.9 20.9 %all-to-all-start = ((bf16[32,4,512]{2,1,0:T(4,128)(2,1)}), bf16[32,4,512]{2,1,0:T(4,128)(2,1)S(1)}, u32[]{:S(2)}, u32[]{:S(2)}) async-start(bf16[32,4,512]{2,1,0:T(4,128)(2,1)} %reshape.36), calls=%async_computation | async-start | bytes 262144 | tf_op jit(solution)/shard_map/all_to_all | solution.py:30
  113.0 191.9 %all-to-all-start.1 = ((bf16[32,512,256]{1,2,0:T(8,128)(2,1)}), bf16[32,512,256]{1,2,0:T(8,128)(2,1)}, u32[]{:S(2)}, u32[]{:S(2)}) async-start(bf16[32,512,256]{1,2,0:T(8,128)(2,1)} %stack.2), calls=%async_computation.1 | async-start | bytes 16777216 | tf_op jit(solution)/shard_map/all_to_all | solution.py:86
  119.2 280.9 %reduce-scatter.2.cloned.1.call-start = ((), (), s32[]{:S(2)}) async-start(), calls=%async_computation.3 | async-start | bytes 7225344 | tf_op jit(solution)/shard_map/reduce_scatter | solution.py:91
  401.1 12.1 %collective-permute-start.2 = (bf16[392,512]{1,0:T(8,128)(2,1)S(1)}, bf16[392,512]{1,0:T(8,128)(2,1)S(1)}, u32[]{:S(2)}, u32[]{:S(2)}) collective-permute-start(bf16[392,512]{1,0:T(8,128)(2,1)S(1)} %constant_dynamic-slice_fusion), channel_id=1, source_target_pairs={{0,1},{1,0},{2,3},{3,2},{4,5},{5,4},{6,7},{7,6},{8,9},{9,8},{10,11... | collective-permute-start | bytes 1204232 | tf_op jit(solution)/shard_map/ppermute | solution.py:23
Sparse Core Ops, SparseCore 0:
  315.7 84.3 reduce-scatter.1
